TPU v7x, 512 devices: a whole 4x4x16 slice. The times are simulated.
512 devices in a mesh: tok: 64 (over z, x), head: 8 (over y, core).
Axes of the slice: x: 4, y: 4, z: 16, core: 2. Of those that a mesh axis runs over, the one named last changes fastest.
Arguments:
- tokens: bfloat16 [32768, 2560], P('tok', 'head'), may hold values from -6 to 6
- query_weight: bfloat16 [2560, 2560], P('tok'), may hold values from -0.125 to 0.125
- keyvalue_weight: bfloat16 [2560, 512], P('tok'), may hold values from -0.125 to 0.125
- output_weight: bfloat16 [2560, 2560], P(None, ('head', 'tok')), may hold values from -0.125 to 0.125
- cache: bfloat16 [2048, 2, 128, 256], P(('tok', 'head')), may hold values from -460 to 460
- page_table: int32 [512, 4], P('tok'), may hold values from 0 to 2047, as said below
- parents: int32 [512, 64], P('tok'), may hold values from 0 to 62, as said below
- cache_len: int32 [512], P('tok'), may hold values from 1 to 448, as said below
- accepted_leaf: int32 [512], P('tok'), may hold values from 0 to 63
Outputs:
- attended: bfloat16 [32768, 2560], P('tok', 'head')
- cache_out: bfloat16 [2048, 2, 128, 256], P(('tok', 'head'))
Inputs may be any that keep to these rules, and one draw needn't show every extreme that they name: `page_table`: for every d, row d names each of the pages d * 4 to d * 4 + 3 exactly once, so request d's pages all lie on device d (devices counted tok-major, head-minor). parents[r, 0] = 0, and parents[r, i] < i for i >= 1. `cache_len`: roughly half of the requests hold at most 128 cached positions, the others more than 320.
All inputs are finite; a program needn't handle non-finite values.
Results may differ from a plain program's by a relative error of at most 0.014.
The roundings to bfloat16 on the way count: a program that leaves them out, or rounds other values in their place, can miss the bound.
Values may be sent and summed in bfloat16 or wider, within the bound.
No kernel may reach another device: no remote copies, remote signals or barrier semaphores. Data moves between devices by JAX's collectives and lax.ppermute only.
A program may use at most 64 MiB of HBM per device.

v0:
```python
import math
import jax
import jax.numpy as jnp
from jax import lax
from jax.sharding import PartitionSpec as P

HQ = 10
HD = 256
DRAFT = 64
PAGE = 128
NPR = 4
WINDOW = 256


def ancestry(parent_row):
    node_ids = jnp.arange(DRAFT, dtype=jnp.int32)
    link = (parent_row[:, None] == node_ids[None, :]).astype(jnp.float32)
    reach = jnp.minimum(link + jnp.eye(DRAFT, dtype=jnp.float32), 1.0)
    for sweep in range((DRAFT - 1).bit_length()):
        reach = jnp.minimum(jnp.dot(reach, reach, precision=lax.Precision.HIGHEST), 1.0)
    depth = (jnp.sum(reach, axis=1) - 1.0).astype(jnp.int32)
    return (reach, depth)


def rotate(values, position):
    half = HD // 4
    freq = jnp.exp(jnp.arange(half, dtype=jnp.float32) * (-2.0 * math.log(10000.0) / (HD // 2)))
    angle = position.astype(jnp.float32)[..., None] * freq
    cosine = jnp.cos(angle)
    sine = jnp.sin(angle)
    first = values[..., :half]
    second = values[..., half : 2 * half]
    return jnp.concatenate(
        [first * cosine - second * sine, second * cosine + first * sine, values[..., 2 * half :]],
        axis=-1,
    )


def attend(queries, cache_keys, cache_values, tree_keys, tree_values, lengths, position, reach):
    window_span = cache_keys.shape[1]
    slot_ids = jnp.arange(window_span, dtype=jnp.int32)
    visible = (slot_ids[None, None, :] < lengths[:, None, None]) & (
        slot_ids[None, None, :] > position[:, :, None] - WINDOW
    )
    cache_scores = jnp.einsum(
        "rnhd,rcd->rhnc", queries, cache_keys, preferred_element_type=jnp.float32
    )
    tree_scores = jnp.einsum(
        "rnhd,rmd->rhnm", queries, tree_keys, preferred_element_type=jnp.float32
    )
    cache_scores = jnp.where(visible[:, None], cache_scores, -1e30)
    tree_scores = jnp.where(reach[:, None] > 0.5, tree_scores, -1e30)
    row_peak = jnp.maximum(jnp.max(cache_scores, axis=-1), jnp.max(tree_scores, axis=-1))[..., None]
    cache_weights = jnp.exp(cache_scores - row_peak)
    tree_weights = jnp.exp(tree_scores - row_peak)
    denominator = jnp.sum(cache_weights, axis=-1, keepdims=True) + jnp.sum(
        tree_weights, axis=-1, keepdims=True
    )
    cache_weights = (cache_weights / denominator).astype(jnp.bfloat16)
    tree_weights = (tree_weights / denominator).astype(jnp.bfloat16)
    result = jnp.einsum(
        "rhnc,rcd->rnhd", cache_weights, cache_values, preferred_element_type=jnp.float32
    )
    result = result + jnp.einsum(
        "rhnm,rmd->rnhd", tree_weights, tree_values, preferred_element_type=jnp.float32
    )
    return result.astype(jnp.bfloat16)


def refresh(logical_pages, length, leaf, reach, depth, new_keys, new_values):
    count = logical_pages.shape[0] * logical_pages.shape[2]
    logical = jnp.transpose(logical_pages, (1, 0, 2, 3)).reshape(2, count, HD)
    slot_ids = jnp.arange(count, dtype=jnp.int32)
    on_path = reach[leaf]
    selector = ((on_path[None, :] > 0.5) & (depth[None, :] == slot_ids[:, None] - length)).astype(
        jnp.float32
    )
    placed_keys = jnp.dot(selector, new_keys.astype(jnp.float32), precision=lax.Precision.HIGHEST)
    placed_values = jnp.dot(
        selector, new_values.astype(jnp.float32), precision=lax.Precision.HIGHEST
    )
    placed = jnp.stack([placed_keys, placed_values]).astype(jnp.bfloat16)
    written = jnp.sum(selector, axis=1) > 0.5
    logical = jnp.where(written[None, :, None], placed, logical)
    return jnp.transpose(
        logical.reshape(2, logical_pages.shape[0], logical_pages.shape[2], HD), (1, 0, 2, 3)
    )


def shards(
    tokens,
    query_weight,
    keyvalue_weight,
    output_weight,
    cache,
    page_table,
    parents,
    cache_len,
    accepted_leaf,
):
    head_count = lax.axis_size("head")
    head_index = lax.axis_index("head")
    tok_index = lax.axis_index("tok")
    requests = parents.shape[0]
    assert requests == head_count
    pages_dev = cache.shape[0]
    part_rows = query_weight.shape[0]
    q_cols = HQ * HD // head_count
    kv_cols = 2 * HD // head_count
    out_cols = output_weight.shape[1]
    wq_piece = lax.dynamic_slice_in_dim(query_weight, head_index * q_cols, q_cols, axis=1)
    wkv_piece = lax.dynamic_slice_in_dim(keyvalue_weight, head_index * kv_cols, kv_cols, axis=1)
    flat = jnp.concatenate([wq_piece.reshape(-1), wkv_piece.reshape(-1), output_weight.reshape(-1)])
    stacked = lax.all_gather(flat, "tok", axis=0, tiled=False)
    tok_count = stacked.shape[0]
    n_q = part_rows * q_cols
    n_kv = part_rows * kv_cols
    wq_cols = stacked[:, :n_q].reshape(tok_count * part_rows, q_cols)
    wkv_cols = stacked[:, n_q : n_q + n_kv].reshape(tok_count * part_rows, kv_cols)
    wo_cols = (
        stacked[:, n_q + n_kv :]
        .reshape(tok_count, HQ * HD, out_cols)
        .transpose(1, 0, 2)
        .reshape(HQ * HD, tok_count * out_cols)
    )
    gathered = lax.all_gather(tokens, "head", axis=1, tiled=True)
    wide = gathered.astype(jnp.float32)
    mean_square = jnp.mean(wide * wide, axis=1, keepdims=True)
    normed = (wide * lax.rsqrt(mean_square + 1e-06)).astype(jnp.bfloat16)
    q_part = jnp.dot(normed, wq_cols, preferred_element_type=jnp.float32)
    kv_part = jnp.dot(normed, wkv_cols, preferred_element_type=jnp.float32)
    both = jnp.concatenate([q_part, kv_part], axis=1)
    mine = lax.all_to_all(both, "head", 0, 1, tiled=True)
    mine = mine.reshape(DRAFT, head_count, q_cols + kv_cols)
    q_pre = mine[:, :, :q_cols].reshape(DRAFT, HQ, HD)
    kv_pre = mine[:, :, q_cols:].reshape(DRAFT, 2 * HD)
    parent_row = lax.dynamic_index_in_dim(parents, head_index, 0, keepdims=False)
    length = lax.dynamic_index_in_dim(cache_len, head_index, 0, keepdims=False)
    leaf = lax.dynamic_index_in_dim(accepted_leaf, head_index, 0, keepdims=False)
    reach, depth = ancestry(parent_row)
    position = length + depth
    queries = (rotate(q_pre, position[:, None]) * HD ** (-0.5)).astype(jnp.bfloat16)
    tree_keys = rotate(kv_pre[:, :HD], position).astype(jnp.bfloat16)
    tree_values = kv_pre[:, HD:].astype(jnp.bfloat16)
    device = tok_index * head_count + head_index
    own_table = (
        lax.dynamic_index_in_dim(page_table, head_index, 0, keepdims=False) - device * pages_dev
    )
    own_pages = jnp.take(cache, own_table, axis=0)
    cache_keys = own_pages[:, 0].reshape(NPR * PAGE, HD)
    cache_values = own_pages[:, 1].reshape(NPR * PAGE, HD)
    result = attend(
        queries[None],
        cache_keys[None],
        cache_values[None],
        tree_keys[None],
        tree_values[None],
        length[None],
        position[None],
        reach[None],
    )
    mixed = lax.all_gather(result.reshape(DRAFT, HQ * HD), "head", axis=0, tiled=True)
    summed = jnp.zeros((mixed.shape[0], wo_cols.shape[1]), jnp.float32)
    for group in range(head_count):
        head_ids = [k for k in range(group, HQ, head_count)]
        if not head_ids:
            continue
        columns = jnp.concatenate([mixed[:, k * HD : (k + 1) * HD] for k in head_ids], axis=1)
        rows = jnp.concatenate([wo_cols[k * HD : (k + 1) * HD] for k in head_ids], axis=0)
        partial_value = jnp.dot(columns, rows, preferred_element_type=jnp.float32)
        summed = summed + partial_value.astype(jnp.bfloat16).astype(jnp.float32)
    attended = summed.astype(jnp.bfloat16)
    new_pages = refresh(own_pages, length, leaf, reach, depth, tree_keys, tree_values)
    matches = (own_table[:, None] == jnp.arange(pages_dev, dtype=jnp.int32)[None, :]).astype(
        jnp.int32
    )
    inverse = jnp.sum(matches * jnp.arange(pages_dev, dtype=jnp.int32)[:, None], axis=0)
    cache_out = jnp.take(new_pages, inverse, axis=0)
    return (attended, cache_out)


def solution(mesh):
    in_specs = (
        P("tok", "head"),
        P("tok", None),
        P("tok", None),
        P(None, ("head", "tok")),
        P(("tok", "head"), None, None, None),
        P("tok", None),
        P("tok", None),
        P("tok"),
        P("tok"),
    )
    out_specs = (P("tok", "head"), P(("tok", "head"), None, None, None))
    return jax.shard_map(shards, mesh=mesh, in_specs=in_specs, out_specs=out_specs, check_vma=False)
```

profile of v0, /device:TPU:1, one launch (start us, length us, event | category | flops | bytes accessed | tf_op | source)
XLA Modules:
  0.0 285.6 jit_solution(11939136876773440064)
XLA Ops:
  9.8 1.2 copy.62
  11.0 1.0 reshape.334
  12.7 1.3 dynamic_slice.29
  15.4 1.2 dynamic_slice.25
  20.4 29.1 %all-gather.6.cloned.1.call-done = bf16[512,2560]{0,1:T(8,128)(2,1)} async-done(((bf16[512,320]{0,1:T(8,128)(2,1)}), bf16[512,2560]{0,1:T(8,128)(2,1)}) %all-gather.6.cloned.1.call-update) | async-done | bytes 2621456 | tf_op jit(solution)/shard_map/all_gather | solution.py:126
  49.5 2.4 fusion
  51.9 146.4 %all-gather.10.cloned.1.call-done = bf16[64,1,28160]{2,1,0:T(2,128)(2,1)} async-done(((bf16[1,1,28160]{2,1,0:T(2,128)(2,1)}), bf16[64,1,28160]{2,1,0:T(2,128)(2,1)}) %all-gather.10.cloned.1.call-update) | async-done | bytes 3604496 | tf_op jit(solution)/shard_map/all_gather | solution.py:114
  198.3 3.5 %copy.97 = bf16[64,1,28160]{2,0,1:T(8,128)(2,1)S(1)} copy(bf16[64,1,28160]{2,1,0:T(2,128)(2,1)} %all-gather.10.cloned.1.call-done) | data formatting | bytes 7208960
  201.7 1.4 fusion.79
  203.1 2.5 reshape.335
  206.0 3.6 %fusion.4 = f32[512,320]{0,1:T(8,128)S(1)} fusion(bf16[2560,320]{1,0:T(8,128)(2,1)} %reshape.335, bf16[512,2560]{0,1:T(8,128)(2,1)} %all-gather.6.cloned.1.call-done, f32[512]{0:T(512)S(1)} %add_rsqrt_fusion), kind=kOutput, calls=%fused_computation.8 | convolution fusion | flops 842792960 | bytes 4917248 | tf_op jit(solution)/shard_map/dot_general | solution.py:130
  210.5 1.2 copy.63
  211.6 12.7 %all-to-all-start = ((f32[8,64,384]{2,1,0:T(8,128)}), f32[8,64,384]{2,1,0:T(8,128)S(1)}, u32[]{:S(2)}, u32[]{:S(2)}) async-start(f32[8,64,384]{2,1,0:T(8,128)} %bitcast.6), calls=%async_computation | async-start | bytes 1572864 | tf_op jit(solution)/shard_map/all_to_all | solution.py:133
  226.4 10.0 %all-to-all-done = f32[8,64,384]{2,1,0:T(8,128)S(1)} async-done(((f32[8,64,384]{2,1,0:T(8,128)}), f32[8,64,384]{2,1,0:T(8,128)S(1)}, u32[]{:S(2)}, u32[]{:S(2)}) %all-to-all-start) | async-done | bytes 786464 | tf_op jit(solution)/shard_map/all_to_all | solution.py:133
  243.5 2.9 %copy.72 = bf16[64,12800]{0,1:T(8,128)(2,1)} copy(bf16[64,12800]{1,0:T(8,128)(2,1)S(1)} %copy-done.1) | data formatting | bytes 3276800 | tf_op jit(solution)/shard_map/slice | solution.py:121
  246.4 7.1 %reshape.342 = bf16[64,2560,5]{0,2,1:T(8,128)(2,1)} reshape(bf16[64,12800]{0,1:T(8,128)(2,1)} %copy.72) | data formatting | bytes 3276800 | tf_op jit(solution)/shard_map/reshape | solution.py:122
  253.5 4.9 %fusion.78 = (bf16[256,64,5]{1,2,0:T(8,128)(2,1)S(1)}, bf16[256,64,5]{1,2,0:T(8,128)(2,1)S(1)}, bf16[256,64,5]{1,2,0:T(8,128)(2,1)S(1)}, bf16[256,64,5]{1,2,0:T(...) fusion(bf16[2560,64,5]{1,2,0:T(8,128)(2,1)} %bitcast.112), kind=kLoop, calls=%fused_computation.143 | loop fusion | bytes 3276800 | tf_op jit(solution)/shard_map/slice | solution.py:169
  258.4 1.5 copy.73
  260.7 1.5 copy.74
  262.9 1.5 copy.75
  265.1 1.5 copy.76
  267.4 1.5 copy.77
  274.4 1.4 fusion.80
  278.1 1.0 fusion.10
  (117 shorter events, 26.9 us)
Async XLA Ops:
  7.2 217.9 %copy-start = (bf16[4,2,128,256]{3,2,1,0:T(8,128)(2,1)S(1)}, bf16[4,2,128,256]{3,2,1,0:T(8,128)(2,1)}, u32[]{:S(2)}) copy-start(bf16[4,2,128,256]{3,2,1,0:T(8,128)(2,1)} %param.15) | copy-start | bytes 1572868
  7.2 12.1 %copy-start.11 = (s32[8,4]{0,1:T(4,128)S(1)}, s32[8,4]{0,1:T(4,128)}, u32[]{:S(2)}) copy-start(s32[8,4]{0,1:T(4,128)} %param.16) | copy-start | bytes 388
  7.2 42.3 %all-gather.6.cloned.1.call-start = ((), (), s32[]{:S(2)}) async-start(), calls=%async_computation.1 | async-start | bytes 2949120 | tf_op jit(solution)/shard_map/all_gather | solution.py:126
  7.9 190.3 %all-gather.10.cloned.1.call-start = ((), (), s32[]{:S(2)}) async-start(), calls=%async_computation.3 | async-start | bytes 7321600 | tf_op jit(solution)/shard_map/all_gather | solution.py:114
  206.0 3.7 %copy-start.2 = (bf16[512,2560]{0,1:T(8,128)(2,1)S(1)}, bf16[512,2560]{0,1:T(8,128)(2,1)}, u32[]{:S(2)}) copy-start(bf16[512,2560]{0,1:T(8,128)(2,1)} %all-gather.6.cloned.1.call-done) | copy-start | bytes 7864324
  211.6 24.9 %all-to-all-start = ((f32[8,64,384]{2,1,0:T(8,128)}), f32[8,64,384]{2,1,0:T(8,128)S(1)}, u32[]{:S(2)}, u32[]{:S(2)}) async-start(f32[8,64,384]{2,1,0:T(8,128)} %bitcast.6), calls=%async_computation | async-start | bytes 1572864 | tf_op jit(solution)/shard_map/all_to_all | solution.py:133
  224.3 50.1 %all-gather.8.cloned.1.call-start = ((), (), s32[]{:S(2)}) async-start(), calls=%async_computation.2 | async-start | bytes 2949120 | tf_op jit(solution)/shard_map/all_gather | solution.py:162
  242.0 1.5 copy-start.1
  270.0 2.9 %copy-start.4 = (bf16[4,2,128,256]{3,2,1,0:T(8,128)(2,1)S(1)}, bf16[4,2,128,256]{3,2,1,0:T(8,128)(2,1)}, u32[]{:S(2)}) copy-start(bf16[4,2,128,256]{3,2,1,0:T(8,128)(2,1)} %get-tuple-element.3) | copy-start | bytes 1572868
  272.3 3.5 %copy-start.9 = (bf16[256,320]{0,1:T(8,128)(2,1)S(1)}, bf16[256,320]{0,1:T(8,128)(2,1)}, u32[]{:S(2)}) copy-start(bf16[256,320]{0,1:T(8,128)(2,1)} %slice.155) | copy-start | bytes 491524
  272.4 3.5 %copy-start.10 = (bf16[256,320]{0,1:T(8,128)(2,1)S(1)}, bf16[256,320]{0,1:T(8,128)(2,1)}, u32[]{:S(2)}) copy-start(bf16[256,320]{0,1:T(8,128)(2,1)} %slice.157) | copy-start | bytes 491524
  273.5 2.8 copy-start.5
  273.5 2.8 copy-start.6
  274.4 2.2 copy-start.7
  274.4 2.2 copy-start.3
  275.9 1.1 copy-start.8
Sparse Core Ops, SparseCore 0:
  10.1 39.3 all-gather.5
  53.1 145.1 all-gather.9
  243.4 27.9 all-gather.7
where the time goes:
time: 287 us; the launch traced here: 286 us
  waiting for transfers between devices  186 us (65%)
  local copies, waits for them, and re-layouts  51.5 us (18%)
  between operations  16.5 us (6%)
  starting transfers between devices  12.8 us (4%)
  matrix products  10.8 us (4%)
  other arithmetic  7.81 us (3%)
    all_gather x1, waiting for transfers between devices, shards(): stacked = lax.all_gather(flat, 'tok', axis=0, tiled=False)  146 us
    all_gather x1, waiting for transfers between devices, shards(): gathered = lax.all_gather(tokens, 'head', axis=1, tiled=True)  29.1 us
    slice x21, local copies, waits for them, and re-layouts, shards(): wo_cols[k * HD:(k + 1) * HD]  19.2 us
    all_to_all x1, starting transfers between devices, shards(): mine = lax.all_to_all(both, 'head', 0, 1, tiled=True)  12.7 us
    all_to_all x1, waiting for transfers between devices, shards(): mine = lax.all_to_all(both, 'head', 0, 1, tiled=True)  10 us
    reshape x1, local copies, waits for them, and re-layouts, shards(): wo_cols = stacked[:, n_q + n_kv:].reshape(tok_count, HQ * HD, out_cols).t...  7.08 us
    unnamed x29, local copies, waits for them, and re-layouts  6.45 us
  transfers between devices with their start and end apart: 4, of which 3 were waited for; matrix products, arithmetic and copies ran while one was open for 16% of the time, Pallas kernels for 0%

commit v1 on v0

--- a/solution.py
+++ b/solution.py
@@ -10,6 +10,11 @@
 PAGE = 128
 NPR = 4
 WINDOW = 256
+
+
+def gather_from_all(x, axis, dim):
+    copies = jnp.concatenate([x] * lax.axis_size(axis), axis=dim)
+    return lax.all_to_all(copies, axis, dim, dim, tiled=True)
 
 
 def ancestry(parent_row):
@@ -123,7 +128,7 @@
         .transpose(1, 0, 2)
         .reshape(HQ * HD, tok_count * out_cols)
     )
-    gathered = lax.all_gather(tokens, "head", axis=1, tiled=True)
+    gathered = gather_from_all(tokens, "head", 1)
     wide = gathered.astype(jnp.float32)
     mean_square = jnp.mean(wide * wide, axis=1, keepdims=True)
     normed = (wide * lax.rsqrt(mean_square + 1e-06)).astype(jnp.bfloat16)

time: 287 us -> 251 us (0.87)
  waiting for transfers between devices: 186 us -> 138 us
  starting transfers between devices: 12.8 us -> 23.2 us
    all_gather x1, waiting for transfers between devices: 146 us -> 103 us  [shards(): stacked = lax.all_gather(flat, 'tok', axis=0, tiled=False)]
    all_gather x1 -> x0, waiting for transfers between devices: 29.1 us -> none  [shards(): gathered = lax.all_gather(tokens, 'head', axis=1, tiled=True)]
    all_to_all x0 -> x1, waiting for transfers between devices: none -> 25 us  [gather_from_all(): return lax.all_to_all(copies, axis, dim, dim, tiled=True)]
    all_to_all x0 -> x1, starting transfers between devices: none -> 10.5 us  [gather_from_all(): return lax.all_to_all(copies, axis, dim, dim, tiled=True)]
    unnamed x29 -> x44, local copies, waits for them, and re-layouts: 6.45 us -> 9.23 us
  transfers between devices with their start and end apart: 4 -> 4, of which waited for: 3 -> 3; matrix products, arithmetic and copies ran while one was open for 16% -> 15% of each run, Pallas kernels for 0% -> 0%
where the time goes in v1:
time: 251 us; the launch traced here: 250 us
  waiting for transfers between devices  138 us (55%)
  local copies, waits for them, and re-layouts  53.8 us (21%)
  starting transfers between devices  23.2 us (9%)
  between operations  16.7 us (7%)
  matrix products  9.73 us (4%)
  other arithmetic  8.16 us (3%)
    all_gather x1, waiting for transfers between devices, shards(): stacked = lax.all_gather(flat, 'tok', axis=0, tiled=False)  103 us
    all_to_all x1, waiting for transfers between devices, gather_from_all(): return lax.all_to_all(copies, axis, dim, dim, tiled=True)  25 us
    slice x21, local copies, waits for them, and re-layouts, shards(): wo_cols[k * HD:(k + 1) * HD]  16.9 us
    all_to_all x1, starting transfers between devices, shards(): mine = lax.all_to_all(both, 'head', 0, 1, tiled=True)  12.7 us
    all_to_all x1, waiting for transfers between devices, shards(): mine = lax.all_to_all(both, 'head', 0, 1, tiled=True)  10.7 us
    all_to_all x1, starting transfers between devices, gather_from_all(): return lax.all_to_all(copies, axis, dim, dim, tiled=True)  10.5 us
    unnamed x44, local copies, waits for them, and re-layouts  9.23 us
    reshape x1, local copies, waits for them, and re-layouts, shards(): wo_cols = stacked[:, n_q + n_kv:].reshape(tok_count, HQ * HD, out_cols).t...  7.08 us
  transfers between devices with their start and end apart: 4, of which 3 were waited for; matrix products, arithmetic and copies ran while one was open for 15% of the time, Pallas kernels for 0%

profile of v1, /device:TPU:1, one launch (start us, length us, event | category | flops | bytes accessed | tf_op | source)
XLA Modules:
  0.0 249.8 jit_solution(2795153089188521090)
XLA Ops:
  9.2 1.2 copy.62
  12.1 1.0 constant_dynamic-update-slice_fusion.7
  13.3 1.6 copy-done.5
  14.9 10.5 %all-to-all-start = ((bf16[512,8,320]{0,2,1:T(8,128)(2,1)}), bf16[512,8,320]{0,2,1:T(8,128)(2,1)S(1)}, u32[]{:S(2)}, u32[]{:S(2)}) async-start(bf16[512,8,320]{0,2,1:T(8,128)(2,1)} %bitcast.123), calls=%async_computation | async-start | bytes 5242880 | tf_op jit(solution)/shard_map/all_to_all | solution.py:17
  32.2 25.0 %all-to-all-done = bf16[512,8,320]{0,2,1:T(8,128)(2,1)S(1)} async-done(((bf16[512,8,320]{0,2,1:T(8,128)(2,1)}), bf16[512,8,320]{0,2,1:T(8,128)(2,1)S(1)}, u32[]{:S(2)}, u32[]{:S(2)}) %all-to-all-start) | async-done | bytes 2621472 | tf_op jit(solution)/shard_map/all_to_all | solution.py:17
  57.8 2.1 fusion.1
  59.9 102.5 %all-gather.7.cloned.1.call-done = bf16[64,1,28160]{2,1,0:T(2,128)(2,1)} async-done(((bf16[1,1,28160]{2,1,0:T(2,128)(2,1)}), bf16[64,1,28160]{2,1,0:T(2,128)(2,1)}) %all-gather.7.cloned.1.call-update) | async-done | bytes 3604496 | tf_op jit(solution)/shard_map/all_gather | solution.py:119
  162.4 3.5 %copy.97 = bf16[64,1,28160]{2,0,1:T(8,128)(2,1)S(1)} copy(bf16[64,1,28160]{2,1,0:T(2,128)(2,1)} %all-gather.7.cloned.1.call-done) | data formatting | bytes 7208960
  165.9 1.9 fusion.75
  167.9 1.2 reshape.350
  169.1 4.1 %reshape.349 = bf16[2560,320]{1,0:T(8,128)(2,1)} reshape(bf16[64,12800]{1,0:T(8,128)(2,1)} %get-tuple-element.16) | data formatting | bytes 3276800 | tf_op jit(solution)/shard_map/reshape | solution.py:123
  173.2 2.7 %fusion.84 = f32[512,320]{0,1:T(8,128)S(1)} fusion(bf16[512,2560]{0,1:T(8,128)(2,1)S(1)} %bitcast.119, bf16[2560,320]{1,0:T(8,128)(2,1)} %reshape.349), kind=kOutput, calls=%fused_computation.157 | convolution fusion | flops 838860800 | bytes 4915200 | tf_op jit(solution)/shard_map/dot_general | solution.py:135
  176.6 1.2 copy.63
  177.7 12.7 %all-to-all-start.1 = ((f32[8,64,384]{2,1,0:T(8,128)}), f32[8,64,384]{2,1,0:T(8,128)S(1)}, u32[]{:S(2)}, u32[]{:S(2)}) async-start(f32[8,64,384]{2,1,0:T(8,128)} %bitcast.8), calls=%async_computation.1 | async-start | bytes 1572864 | tf_op jit(solution)/shard_map/all_to_all | solution.py:138
  191.9 10.7 %all-to-all-done.1 = f32[8,64,384]{2,1,0:T(8,128)S(1)} async-done(((f32[8,64,384]{2,1,0:T(8,128)}), f32[8,64,384]{2,1,0:T(8,128)S(1)}, u32[]{:S(2)}, u32[]{:S(2)}) %all-to-all-start.1) | async-done | bytes 786464 | tf_op jit(solution)/shard_map/all_to_all | solution.py:138
  209.6 2.9 %copy.72 = bf16[64,12800]{0,1:T(8,128)(2,1)} copy(bf16[64,12800]{1,0:T(8,128)(2,1)S(1)} %copy-done.4) | data formatting | bytes 3276800 | tf_op jit(solution)/shard_map/slice | solution.py:126
  212.6 7.1 %reshape.356 = bf16[64,2560,5]{0,2,1:T(8,128)(2,1)} reshape(bf16[64,12800]{0,1:T(8,128)(2,1)} %copy.72) | data formatting | bytes 3276800 | tf_op jit(solution)/shard_map/reshape | solution.py:127
  219.6 5.0 %fusion.74 = (bf16[256,64,5]{1,2,0:T(8,128)(2,1)}, bf16[256,64,5]{1,2,0:T(8,128)(2,1)}, bf16[256,64,5]{1,2,0:T(8,128)(2,1)}, bf16[256,64,5]{1,2,0:T(8,128)(2,1)}...) fusion(bf16[2560,64,5]{1,2,0:T(8,128)(2,1)} %bitcast.116), kind=kLoop, calls=%fused_computation.149 | loop fusion | bytes 3276800 | tf_op jit(solution)/shard_map/slice | solution.py:174
  224.6 1.5 copy.82
  226.8 1.5 copy.81
  229.0 1.5 copy.80
  231.3 1.5 copy.79
  238.2 1.4 fusion.76
  242.0 1.0 fusion.6
  (133 shorter events, 28.0 us)
Async XLA Ops:
  7.2 183.4 %copy-start = (bf16[4,2,128,256]{3,2,1,0:T(8,128)(2,1)S(1)}, bf16[4,2,128,256]{3,2,1,0:T(8,128)(2,1)}, u32[]{:S(2)}) copy-start(bf16[4,2,128,256]{3,2,1,0:T(8,128)(2,1)} %param.15) | copy-start | bytes 1572868
  7.2 5.9 %copy-start.2 = (bf16[512,320]{0,1:T(8,128)(2,1)S(1)}, bf16[512,320]{0,1:T(8,128)(2,1)}, u32[]{:S(2)}) copy-start(bf16[512,320]{0,1:T(8,128)(2,1)} %param.11) | copy-start | bytes 983044
  7.2 155.3 %all-gather.7.cloned.1.call-start = ((), (), s32[]{:S(2)}) async-start(), calls=%async_computation.3 | async-start | bytes 7321600 | tf_op jit(solution)/shard_map/all_gather | solution.py:119
  13.3 1.6 copy-start.5
  14.8 11.6 %copy-start.14 = (s32[8]{0:T(128)S(1)}, s32[8]{0:T(128)}, u32[]{:S(2)}) copy-start(s32[8]{0:T(128)} %param.19) | copy-start | bytes 100
  14.9 13.6 %copy-start.15 = (s32[8]{0:T(128)S(1)}, s32[8]{0:T(128)}, u32[]{:S(2)}) copy-start(s32[8]{0:T(128)} %param.18) | copy-start | bytes 100
  14.9 15.6 %copy-start.13 = (s32[8,4]{0,1:T(4,128)S(1)}, s32[8,4]{0,1:T(4,128)}, u32[]{:S(2)}) copy-start(s32[8,4]{0,1:T(4,128)} %param.16) | copy-start | bytes 388
  14.9 42.3 %all-to-all-start = ((bf16[512,8,320]{0,2,1:T(8,128)(2,1)}), bf16[512,8,320]{0,2,1:T(8,128)(2,1)S(1)}, u32[]{:S(2)}, u32[]{:S(2)}) async-start(bf16[512,8,320]{0,2,1:T(8,128)(2,1)} %bitcast.123), calls=%async_computation | async-start | bytes 5242880 | tf_op jit(solution)/shard_map/all_to_all | solution.py:17
  167.9 5.4 %copy-start.3 = (bf16[512,8,320]{0,2,1:T(8,128)(2,1)S(1)}, bf16[512,8,320]{0,2,1:T(8,128)(2,1)}, u32[]{:S(2)}) copy-start(bf16[512,8,320]{0,2,1:T(8,128)(2,1)} %fusion.1) | copy-start | bytes 7864324
  173.2 2.7 %copy-start.7 = (bf16[2560,64]{1,0:T(8,128)(2,1)S(1)}, bf16[2560,64]{1,0:T(8,128)(2,1)}, u32[]{:S(2)}) copy-start(bf16[2560,64]{1,0:T(8,128)(2,1)} %reshape.350) | copy-start | bytes 983044
  177.7 24.9 %all-to-all-start.1 = ((f32[8,64,384]{2,1,0:T(8,128)}), f32[8,64,384]{2,1,0:T(8,128)S(1)}, u32[]{:S(2)}, u32[]{:S(2)}) async-start(f32[8,64,384]{2,1,0:T(8,128)} %bitcast.8), calls=%async_computation.1 | async-start | bytes 1572864 | tf_op jit(solution)/shard_map/all_to_all | solution.py:138
  190.4 47.8 %all-gather.5.cloned.1.call-start = ((), (), s32[]{:S(2)}) async-start(), calls=%async_computation.2 | async-start | bytes 2949120 | tf_op jit(solution)/shard_map/all_gather | solution.py:167
  208.2 1.5 copy-start.4
  234.5 2.2 copy-start.8
  238.2 2.2 copy-start.6
  240.0 1.0 copy-start.12
  240.4 0.9 copy-start.11
  240.7 0.9 copy-start.10
  241.0 1.0 copy-start.9
  241.0 2.0 copy-start.1
Sparse Core Ops, SparseCore 0:
  12.2 150.2 all-gather.6
  209.5 27.9 all-gather.4
